TPU v7x, 256 devices: a whole 4x4x8 slice. The times are simulated.
256 devices in a mesh: seq: 32 (over x, y, z_hi), tp: 8 (over z_lo, core).
Axes of the slice: x: 4, y: 4, z: 8 (z_hi: 2, z_lo: 4; z = z_hi * 4 + z_lo), core: 2. Of those that a mesh axis runs over, the one named last changes fastest.
Arguments:
- prefill_tokens: bfloat16 [8192, 4608], P('seq'), may hold values from -6 to 6
- decode_tokens: bfloat16 [64, 4608], replicated, may hold values from -6 to 6
- norm_gain: float32 [4608], replicated, may hold values from 0.1 to 1.9
- w_query: bfloat16 [4608, 4096], P('seq', 'tp'), may hold values from -2.1213203 to 2.1213203
- w_key: bfloat16 [4608, 2048], P('seq', 'tp'), may hold values from -0.09375 to 0.09375
- w_value: bfloat16 [4608, 2048], P('seq', 'tp'), may hold values from -0.09375 to 0.09375
- w_output: bfloat16 [4096, 4608], P('seq', 'tp'), may hold values from -0.09375 to 0.09375
- prefill_lengths: int32 [6], replicated, may hold values from 1 to 6144, 8192 in all
- context_lengths: int32 [2], replicated, may hold values from 2048 to 8192, as said below
- tail_lengths: int32 [32], replicated, may hold values from 1 to 256, as said below
- tail_slots: int32 [32], replicated, may hold values from 0 to 63, as said below
- cache_keys: bfloat16 [2, 8192, 2048], P(None, 'seq', 'tp'), may hold values from -6 to 6
- cache_values: bfloat16 [2, 8192, 2048], P(None, 'seq', 'tp'), may hold values from -6 to 6
- tail_keys: bfloat16 [64, 256, 2048], P('seq', None, 'tp'), may hold values from -6 to 6
- tail_values: bfloat16 [64, 256, 2048], P('seq', None, 'tp'), may hold values from -6 to 6
Outputs:
- prefill_out: bfloat16 [8192, 4608], P('seq', 'tp')
- decode_out: bfloat16 [64, 4608], P('seq', 'tp')
Inputs may be any that keep to these rules, and one draw needn't show every extreme that they name: `prefill_lengths`: the prompts fill all 8192 prefill tokens; the longest has exactly 6144. `context_lengths`: some prompt has exactly 8192 cached positions. `tail_lengths`: some sample has exactly 256 tail positions. `tail_slots`: distinct slot numbers; slot q lies with seq index q // 2; in every draw all slots of some seq index are used.
All inputs are finite; a program needn't handle non-finite values.
Results may differ from a plain program's by a relative error of at most 0.019.
Values may be sent and summed in bfloat16 or wider, within the bound.
No kernel may reach another device: no remote copies, remote signals or barrier semaphores. Data moves between devices by JAX's collectives and lax.ppermute only.
A program may use at most 128 MiB of HBM per device.

v0:
```python
import math
import jax
import jax.numpy as jnp
from jax import lax
from jax.sharding import PartitionSpec as P

HEAD = 128
SAMPLES = 16
NEW = 2
SOFTCAP = 50.0
QUERY_SCALE = 144.0 ** (-0.5)
NORM_EPSILON = 1e-06
ROPE_BASE = 10000.0


def combined_all(shard, axis, combine):
    everything = jax.tree.map(
        lambda part, kind: lax.all_gather(part.astype(kind), axis),
        shard,
        jax.tree.map(lambda a: jnp.bfloat16 if a.dtype == jnp.float32 else a.dtype, shard),
    )

    def take(k):
        return jax.tree.map(lambda part, own: part[k].astype(own.dtype), everything, shard)

    return lax.fori_loop(
        1, lax.axis_size(axis), lambda k, so_far: combine(so_far, take(k)), take(0)
    )


def rms_norm(inputs, norm_gain):
    values = inputs.astype(jnp.float32)
    mean_sq = jnp.mean(values * values, axis=-1, keepdims=True)
    return (values * lax.rsqrt(mean_sq + NORM_EPSILON) * norm_gain).astype(jnp.bfloat16)


def rotate(values, positions):
    half_size = values.shape[-1] // 2
    exponent = jnp.arange(half_size, dtype=jnp.float32) * (2.0 / values.shape[-1])
    frequency = ROPE_BASE ** (-exponent)
    angles = positions.astype(jnp.float32)[:, None] * frequency[None, :]
    cosine = jnp.cos(angles)[:, None, :]
    sine_part = jnp.sin(angles)[:, None, :]
    lower_half = values[..., :half_size]
    upper_half = values[..., half_size:]
    return jnp.concatenate(
        [
            lower_half * cosine - upper_half * sine_part,
            upper_half * cosine + lower_half * sine_part,
        ],
        axis=-1,
    )


def soft_cap(scores):
    return SOFTCAP * jnp.tanh(scores / SOFTCAP)


def prefill_positions(prefill_lengths, token_index):
    prompt_ends = jnp.cumsum(prefill_lengths)
    passed = token_index[:, None] >= prompt_ends[None, :]
    segment = jnp.sum(passed.astype(jnp.int32), axis=1)
    start_at = jnp.sum(jnp.where(passed, prefill_lengths[None, :], 0), axis=1)
    return (segment, token_index - start_at)


def lookup(table, indices):
    entries = jnp.arange(table.shape[0], dtype=jnp.int32)
    return jnp.sum(jnp.where(indices[:, None] == entries[None, :], table[None, :], 0), axis=1)


def combine(earlier, later):
    return (earlier[0] + later[0], earlier[1] + later[1])


def partial_softmax(scores, allowed, value_block, form):
    weights = jnp.where(allowed, jnp.exp(scores), 0.0)
    total_sum = jnp.sum(weights, axis=-1)
    mixed_out = jnp.einsum(
        form, weights.astype(jnp.bfloat16), value_block, preferred_element_type=jnp.float32
    )
    return (total_sum, mixed_out)


def shards(
    prefill_tokens,
    decode_tokens,
    norm_gain,
    w_query,
    w_key,
    w_value,
    w_output,
    prefill_lengths,
    context_lengths,
    tail_lengths,
    tail_slots,
    cache_keys,
    cache_values,
    tail_keys,
    tail_values,
):
    seq_count = lax.axis_size("seq")
    seq_index = lax.axis_index("seq")
    pf_rows = prefill_tokens.shape[0]
    dec_total = decode_tokens.shape[0]
    dec_rows = dec_total // seq_count
    q_heads = w_query.shape[1] // HEAD
    kv_heads = w_key.shape[1] // HEAD
    group_size = q_heads // kv_heads
    token_index = seq_index * pf_rows + jnp.arange(pf_rows, dtype=jnp.int32)
    query_seg, pf_positions = prefill_positions(prefill_lengths, token_index)
    row_ids = jnp.arange(dec_total, dtype=jnp.int32)
    sample_ids = row_ids // NEW
    dec_positions = (
        lookup(context_lengths, sample_ids // SAMPLES)
        + lookup(tail_lengths, sample_ids)
        + row_ids % NEW
    )
    positions = jnp.concatenate([pf_positions, dec_positions], axis=0)
    normed = rms_norm(jnp.concatenate([prefill_tokens, decode_tokens], axis=0), norm_gain)
    row_total = normed.shape[0]
    pieces = (
        lax.all_gather(w_query, "seq", axis=0, tiled=True),
        lax.all_gather(w_key, "seq", axis=0, tiled=True),
        lax.all_gather(w_value, "seq", axis=0, tiled=True),
    )
    columns = normed
    query_all, key_all, value_all = tuple(
        (jnp.dot(columns, piece_part, preferred_element_type=jnp.float32) for piece_part in pieces)
    )
    query_all = (
        rotate(query_all.reshape(row_total, q_heads, HEAD), positions) * QUERY_SCALE
    ).astype(jnp.bfloat16)
    key_all = (
        rotate(key_all.reshape(row_total, kv_heads, HEAD), positions)
        .astype(jnp.bfloat16)
        .reshape(row_total, -1)
    )
    value_all = value_all.astype(jnp.bfloat16)
    pf_query = query_all[:pf_rows].reshape(pf_rows, kv_heads, group_size, HEAD)
    pf_key = key_all[:pf_rows]
    pf_value = value_all[:pf_rows]
    query_last = token_index[pf_rows - 1]
    prompt_first = token_index[0] - pf_positions[0]
    start_state = (
        jnp.zeros((pf_rows, kv_heads, group_size), jnp.float32),
        jnp.zeros((pf_rows, kv_heads, group_size, HEAD), jnp.float32),
    )
    key_piece = lax.all_gather(pf_key, "seq", axis=0, tiled=True)
    value_piece = lax.all_gather(pf_value, "seq", axis=0, tiled=True)
    piece_len = key_piece.shape[0]
    block_len = math.gcd(512, piece_len)

    def one_block(block_step, carry_state):
        begin = block_step * block_len
        key_block = lax.dynamic_slice_in_dim(
            key_piece, block_step * block_len, block_len, 0
        ).reshape(block_len, kv_heads, HEAD)
        value_block = lax.dynamic_slice_in_dim(
            value_piece, block_step * block_len, block_len, 0
        ).reshape(block_len, kv_heads, HEAD)

        def compute(state_in):
            key_index = begin + jnp.arange(block_len, dtype=jnp.int32)
            key_seg, unused_pos = prefill_positions(prefill_lengths, key_index)
            allowed = (query_seg[:, None] == key_seg[None, :]) & (
                key_index[None, :] <= token_index[:, None]
            )
            scores = soft_cap(
                jnp.einsum(
                    "qgjd,kgd->qgjk", pf_query, key_block, preferred_element_type=jnp.float32
                )
            )
            weights = jnp.where(allowed[:, None, None, :], jnp.exp(scores), 0.0)
            total_sum = state_in[0] + jnp.sum(weights, axis=-1)
            mixed_out = state_in[1] + jnp.einsum(
                "qgjk,kgd->qgjd",
                weights.astype(jnp.bfloat16),
                value_block,
                preferred_element_type=jnp.float32,
            )
            return (total_sum, mixed_out)

        is_live = (begin <= query_last) & (begin + block_len > prompt_first)
        return lax.cond(is_live, compute, lambda state_in: state_in, carry_state)

    pf_state = lax.fori_loop(0, piece_len // block_len, one_block, start_state)
    pf_attn = (
        (pf_state[1] / pf_state[0][..., None]).astype(jnp.bfloat16).reshape(pf_rows, q_heads * HEAD)
    )
    dec_query = query_all[pf_rows:]
    dec_key = key_all[pf_rows:]
    dec_value = value_all[pf_rows:]
    prompt_count = cache_keys.shape[0]
    ctx_rows = cache_keys.shape[1]
    prompt_queries = dec_query.reshape(prompt_count, SAMPLES * NEW, kv_heads, group_size, HEAD)
    cache_k = cache_keys.reshape(prompt_count, ctx_rows, kv_heads, HEAD)
    cache_v = cache_values.reshape(prompt_count, ctx_rows, kv_heads, HEAD)
    cache_pos = seq_index * ctx_rows + jnp.arange(ctx_rows, dtype=jnp.int32)
    cache_allowed = (cache_pos[None, :] < context_lengths[:, None])[:, None, None, None, :]
    cache_scores = soft_cap(
        jnp.einsum("prgjd,pcgd->prgjc", prompt_queries, cache_k, preferred_element_type=jnp.float32)
    )
    prefix_part = partial_softmax(cache_scores, cache_allowed, cache_v, "prgjc,pcgd->prgjd")
    prefix_part = (
        prefix_part[0].reshape(dec_total, kv_heads, group_size),
        prefix_part[1].reshape(dec_total, kv_heads, group_size, HEAD),
    )
    slot_count = tail_keys.shape[0]
    tail_len = tail_keys.shape[1]
    sample_total = tail_slots.shape[0]
    local_slots = seq_index * slot_count + jnp.arange(slot_count, dtype=jnp.int32)
    owner = tail_slots[None, :] == local_slots[:, None]
    slot_queries = jnp.dot(
        owner.astype(jnp.bfloat16),
        dec_query.reshape(sample_total, NEW * q_heads * HEAD),
        preferred_element_type=jnp.float32,
    )
    slot_queries = slot_queries.astype(jnp.bfloat16).reshape(
        slot_count, NEW, kv_heads, group_size, HEAD
    )
    slot_lengths = jnp.sum(jnp.where(owner, tail_lengths[None, :], 0), axis=1)
    tail_allowed = (jnp.arange(tail_len, dtype=jnp.int32)[None, :] < slot_lengths[:, None])[
        :, None, None, None, :
    ]
    slot_keys = tail_keys.reshape(slot_count, tail_len, kv_heads, HEAD)
    slot_values = tail_values.reshape(slot_count, tail_len, kv_heads, HEAD)
    tail_scores = soft_cap(
        jnp.einsum("sngjd,stgd->sngjt", slot_queries, slot_keys, preferred_element_type=jnp.float32)
    )
    slot_part = partial_softmax(tail_scores, tail_allowed, slot_values, "sngjt,stgd->sngjd")
    owned_by = owner.T
    tail_sum = jnp.sum(jnp.where(owned_by[:, :, None, None, None], slot_part[0][None], 0.0), axis=1)
    tail_mix = jnp.sum(
        jnp.where(owned_by[:, :, None, None, None, None], slot_part[1][None], 0.0), axis=1
    )
    tail_part = (
        tail_sum.reshape(dec_total, kv_heads, group_size),
        tail_mix.reshape(dec_total, kv_heads, group_size, HEAD),
    )
    partials = combine(prefix_part, tail_part)
    combined = combined_all(partials, "seq", combine)
    merged = tuple(
        (lax.dynamic_slice_in_dim(member, seq_index * dec_rows, dec_rows, 0) for member in combined)
    )
    own_rows = seq_index * dec_rows + jnp.arange(dec_rows, dtype=jnp.int32)
    own_query = lax.dynamic_slice_in_dim(dec_query, seq_index * dec_rows, dec_rows, 0).reshape(
        dec_rows, kv_heads, group_size, HEAD
    )
    near_ids = (own_rows // NEW)[:, None] * NEW + jnp.arange(NEW, dtype=jnp.int32)[None, :]
    near_keys = jnp.take(dec_key, near_ids, axis=0).reshape(dec_rows, NEW, kv_heads, HEAD)
    near_values = jnp.take(dec_value, near_ids, axis=0).reshape(dec_rows, NEW, kv_heads, HEAD)
    near_allowed = (jnp.arange(NEW, dtype=jnp.int32)[None, :] <= (own_rows % NEW)[:, None])[
        :, None, None, :
    ]
    near_scores = soft_cap(
        jnp.einsum("rgjd,rmgd->rgjm", own_query, near_keys, preferred_element_type=jnp.float32)
    )
    near_part = partial_softmax(near_scores, near_allowed, near_values, "rgjm,rmgd->rgjd")
    finished = combine(merged, near_part)
    dec_attn = (
        (finished[1] / finished[0][..., None])
        .astype(jnp.bfloat16)
        .reshape(dec_rows, q_heads * HEAD)
    )
    attn_rows = jnp.concatenate([pf_attn, dec_attn], axis=0)
    heads_all = lax.all_gather(attn_rows, "tp", axis=1, tiled=True)
    columns = heads_all
    projected = jnp.dot(
        columns,
        lax.all_gather(w_output, "seq", axis=0, tiled=True),
        preferred_element_type=jnp.float32,
    )
    projected = projected.astype(jnp.bfloat16)
    return (projected[:pf_rows], projected[pf_rows:])


def solution(mesh):
    return jax.shard_map(
        shards,
        mesh=mesh,
        in_specs=(
            P("seq", None),
            P(),
            P(),
            P("seq", "tp"),
            P("seq", "tp"),
            P("seq", "tp"),
            P("seq", "tp"),
            P(),
            P(),
            P(),
            P(),
            P(None, "seq", "tp"),
            P(None, "seq", "tp"),
            P("seq", None, "tp"),
            P("seq", None, "tp"),
        ),
        out_specs=(P("seq", "tp"), P("seq", "tp")),
        check_vma=False,
    )
```

profile of v0, /device:TPU:2, one launch (start us, length us, event | category | flops | bytes accessed | tf_op | source)
XLA Modules:
  0.0 830.4 jit_solution(975228371402905375)
XLA Ops:
  9.5 2.5 fusion.4
  12.0 94.7 %all-gather.15.cloned.1.call-done = bf16[4608,256]{1,0:T(8,128)(2,1)} async-done(((bf16[144,256]{1,0:T(8,128)(2,1)}), bf16[4608,256]{1,0:T(8,128)(2,1)}) %all-gather.15.cloned.1.call-update) | async-done | bytes 2359312 | tf_op jit(solution)/shard_map/all_gather | solution.py:125
  106.7 2.6 convolution_convert_fusion.1
  111.3 86.3 %all-gather.9.cloned.1.call-done = bf16[4608,256]{1,0:T(8,128)(2,1)} async-done(((bf16[144,256]{1,0:T(8,128)(2,1)}), bf16[4608,256]{1,0:T(8,128)(2,1)}) %all-gather.9.cloned.1.call-update) | async-done | bytes 2359312 | tf_op jit(solution)/shard_map/all_gather | solution.py:124
  197.6 2.8 fusion.58
  202.4 1.7 reshape.524
  204.1 1.7 reshape.528
  205.8 1.7 reshape.532
  207.5 1.7 reshape.530
  210.2 101.4 %all-gather.13.cloned.1.call-done = bf16[4608,512]{1,0:T(8,128)(2,1)} async-done(((bf16[144,512]{1,0:T(8,128)(2,1)}), bf16[4608,512]{1,0:T(8,128)(2,1)}) %all-gather.13.cloned.1.call-update) | async-done | bytes 4718608 | tf_op jit(solution)/shard_map/all_gather | solution.py:123
  311.6 5.1 fusion.56
  316.7 1.3 reshape.520
  326.4 102.9 %all_gather.34 = bf16[32,64,2,2]{1,3,2,0:T(2,128)(2,1)S(1)} all-gather(bf16[1,64,2,2]{1,3,2,0:T(2,128)(2,1)S(1)} %add_convert_fusion.2), channel_id=1, replica_groups=mesh['seq'=32,'tp'=8] {'seq'}, dimensions={0}, use_global_device_ids=true | all-gather | bytes 16896 | tf_op jit(solution)/shard_map/all_gather | solution.py:18
  429.6 6.4 copy.159
  436.0 108.2 %all-gather.11.cloned.1.call-done = bf16[8192,256]{0,1:T(8,128)(2,1)} async-done(((bf16[256,256]{0,1:T(8,128)(2,1)}), bf16[8192,256]{0,1:T(8,128)(2,1)}) %all-gather.11.cloned.1.call-update) | async-done | bytes 4194320 | tf_op jit(solution)/shard_map/all_gather | solution.py:149
  544.3 14.0 %while.34 = (s32[]{:T(128)}, f32[256,2,2]{0,2,1:T(2,128)S(1)}, f32[256,2,2,128]{3,0,2,1:T(8,128)S(1)}, s32[]{:T(128)}, s32[]{:T(128)}, /*index=5*/s32[256]{0:T(2...) while((s32[]{:T(128)}, f32[256,2,2]{0,2,1:T(2,128)S(1)}, ...), condition=%wide.region_12.13_spmd.clone, body=%wide.region_6.12_spmd.clone.sunk | while | flops 271590688 | bytes 5275049 | solution.py:187
  547.7 3.1 conditional.3
  547.7 1.1 constant_dynamic-slice_fusion
  549.3 0.9 fusion.60
  558.6 74.9 %all-gather.19.cloned.1.call-done = bf16[32,64,2,2,128]{4,1,3,2,0:T(8,128)(2,1)} async-done(((bf16[1,64,2,2,128]{4,1,3,2,0:T(8,128)(2,1)}), bf16[32,64,2,2,128]{4,1,3,2,0:T(8,128)(2,1)}) %all-gather.19.cloned.1.call-update) | async-done | bytes 2097168 | tf_op jit(solution)/shard_map/all_gather | solution.py:18
  634.4 33.7 %while.33 = (s32[]{:T(128)}, f32[64,2,2]{0,2,1:T(2,128)S(1)}, f32[64,2,2,128]{3,2,1,0:T(2,128)S(1)}, bf16[32,64,2,2]{1,3,2,0:T(2,128)(2,1)S(1)}, bf16[32,64,2,2,...) while((s32[]{:T(128)}, f32[64,2,2]{0,2,1:T(2,128)S(1)}, f32[64,2,2,128]{3,2,1,0:T(2,128)S(1)}, ...), condition=%wide.region_19.20_spmd, body=%wide.region_18.19_spmd.sunk | while | flops 66053 | bytes 461447 | solution.py:26
  634.5 0.9 constant_dynamic-slice_fusion.5
  636.6 0.9 constant_dynamic-slice_fusion.5
  643.1 0.9 constant_dynamic-slice_fusion.5
  644.2 0.9 constant_dynamic-slice_fusion.5
  645.3 0.9 constant_dynamic-slice_fusion.5
  652.9 0.9 constant_dynamic-slice_fusion.5
  654.0 0.9 constant_dynamic-slice_fusion.5
  669.5 104.2 %all-gather.23.cloned.1.call-done = bf16[4096,576]{0,1:T(8,128)(2,1)} async-done(((bf16[128,576]{0,1:T(8,128)(2,1)}), bf16[4096,576]{0,1:T(8,128)(2,1)}) %all-gather.23.cloned.1.call-update) | async-done | bytes 4718608 | tf_op jit(solution)/shard_map/all_gather | solution.py:271
  773.7 42.5 %all-gather.21.cloned.1.call-done = bf16[258,4096]{0,1:T(8,128)(2,1)} async-done(((bf16[258,512]{0,1:T(8,128)(2,1)}), bf16[258,4096]{0,1:T(8,128)(2,1)}) %all-gather.21.cloned.1.call-update) | async-done | bytes 2113552 | tf_op jit(solution)/shard_map/all_gather | solution.py:267
  816.1 5.9 convolution_convert_fusion
  822.7 0.9 copy.180
  (243 shorter events, 46.4 us)
Async XLA Ops:
  7.2 99.5 %copy-start.2 = (bf16[64,4608]{1,0:T(8,128)(2,1)S(1)}, bf16[64,4608]{1,0:T(8,128)(2,1)}, u32[]{:S(2)}) copy-start(bf16[64,4608]{1,0:T(8,128)(2,1)} %param.24) | copy-start | bytes 1769476
  7.2 99.5 %copy-start = (bf16[256,4608]{1,0:T(8,128)(2,1)S(1)}, bf16[256,4608]{1,0:T(8,128)(2,1)}, u32[]{:S(2)}) copy-start(bf16[256,4608]{1,0:T(8,128)(2,1)} %param.23) | copy-start | bytes 7077892
  7.2 99.5 %copy-start.10 = (f32[4608]{0:T(1024)S(1)}, f32[4608]{0:T(1024)}, u32[]{:S(2)}) copy-start(f32[4608]{0:T(1024)} %param.25) | copy-start | bytes 55300
  7.2 99.5 %all-gather.15.cloned.1.call-start = ((), (), s32[]{:S(2)}) async-start(), calls=%async_computation.3 | async-start | bytes 2433024 | tf_op jit(solution)/shard_map/all_gather | solution.py:125
  7.9 189.6 %all-gather.9.cloned.1.call-start = ((), (), s32[]{:S(2)}) async-start(), calls=%async_computation | async-start | bytes 2433024 | tf_op jit(solution)/shard_map/all_gather | solution.py:124
  8.7 302.9 %all-gather.13.cloned.1.call-start = ((), (), s32[]{:S(2)}) async-start(), calls=%async_computation.2 | async-start | bytes 4866048 | tf_op jit(solution)/shard_map/all_gather | solution.py:123
  9.4 420.2 %all-gather.17.cloned.1.call-start = ((), (), s32[]{:S(2)}) async-start(), calls=%async_computation.4 | async-start | bytes 4325376 | tf_op jit(solution)/shard_map/all_gather | solution.py:150
  12.0 98.1 %copy-start.9 = (s32[6]{0:T(128)S(1)}, s32[6]{0:T(128)}, u32[]{:S(2)}) copy-start(s32[6]{0:T(128)} %param.30) | copy-start | bytes 76
  12.0 98.3 %copy-start.6 = (s32[2]{0:T(128)S(1)}, s32[2]{0:T(128)}, u32[]{:S(2)}) copy-start(s32[2]{0:T(128)} %param.31) | copy-start | bytes 28
  12.0 98.4 %copy-start.7 = (s32[32]{0:T(128)S(1)}, s32[32]{0:T(128)}, u32[]{:S(2)}) copy-start(s32[32]{0:T(128)} %param.32) | copy-start | bytes 388
  110.0 434.2 %all-gather.11.cloned.1.call-start = ((), (), s32[]{:S(2)}) async-start(), calls=%async_computation.1 | async-start | bytes 4325376 | tf_op jit(solution)/shard_map/all_gather | solution.py:149
  200.4 9.4 %copy-start.8 = (s32[32]{0:T(128)S(1)}, s32[32]{0:T(128)}, u32[]{:S(2)}) copy-start(s32[32]{0:T(128)} %param.33) | copy-start | bytes 388
  202.3 431.1 %all-gather.19.cloned.1.call-start = ((), (), s32[]{:S(2)}) async-start(), calls=%async_computation.5 | async-start | bytes 2162688 | tf_op jit(solution)/shard_map/all_gather | solution.py:18
  318.4 1.0 copy-start.5
  318.4 1.2 copy-start.4
  318.4 1.6 copy-start.3
  318.5 1.9 copy-start.1
  318.6 4.8 copy-start.11
  321.2 452.4 %all-gather.23.cloned.1.call-start = ((), (), s32[]{:S(2)}) async-start(), calls=%async_computation.7 | async-start | bytes 4866048 | tf_op jit(solution)/shard_map/all_gather | solution.py:271
  322.0 494.1 %all-gather.21.cloned.1.call-start = ((), (), s32[]{:S(2)}) async-start(), calls=%async_computation.6 | async-start | bytes 3538944 | tf_op jit(solution)/shard_map/all_gather | solution.py:267
Sparse Core Ops, SparseCore 0:
  11.4 95.2 all-gather.14
  110.1 87.4 all-gather.8
  201.0 110.5 all-gather.12
  314.9 105.5 all-gather.16
  423.6 120.6 all-gather.10
  548.1 85.2 all-gather.18
  636.7 136.9 all-gather.22
  775.5 40.6 all-gather.20
where the time goes:
time: 833 us; the launch traced here: 830 us
  waiting for transfers between devices  615 us (74%)
  blocking collectives  103 us (12%)
  local copies, waits for them, and re-layouts  49.4 us (6%)
  matrix products  19.5 us (2%)
  other arithmetic  16.4 us (2%)
  between operations  15.8 us (2%)
  loops' own time  11.1 us (1%)
    all_gather x1, waiting for transfers between devices, shards(): key_piece = lax.all_gather(pf_key, 'seq', axis=0, tiled=True)  108 us
    all_gather x1, waiting for transfers between devices, shards(): lax.all_gather(w_output, 'seq', axis=0, tiled=True)  104 us
    all_gather x1, blocking collectives, combined_all(): lax.all_gather(part.astype(kind), axis)  103 us
    all_gather x1, waiting for transfers between devices, shards(): lax.all_gather(w_query, 'seq', axis=0, tiled=True)  101 us
    all_gather x1, waiting for transfers between devices, shards(): lax.all_gather(w_value, 'seq', axis=0, tiled=True)  94.7 us
    all_gather x1, waiting for transfers between devices, shards(): lax.all_gather(w_key, 'seq', axis=0, tiled=True)  86.3 us
    all_gather x1, waiting for transfers between devices, combined_all(): lax.all_gather(part.astype(kind), axis)  74.9 us
    all_gather x1, waiting for transfers between devices, shards(): heads_all = lax.all_gather(attn_rows, 'tp', axis=1, tiled=True)  42.5 us
  transfers between devices with their start and end apart: 8, of which 7 were waited for; matrix products, arithmetic and copies ran while one was open for 9% of the time, Pallas kernels for 0%

commit v1 on v0

--- a/solution.py
+++ b/solution.py
@@ -121,7 +121,9 @@
     row_total = normed.shape[0]
     pieces = (
         lax.all_gather(w_query, "seq", axis=0, tiled=True),
-        lax.all_gather(w_key, "seq", axis=0, tiled=True),
+        jnp.concatenate(
+            jax.lax.all_to_all(jnp.stack([w_key] * jax.lax.axis_size("seq"), 0), "seq", 0, 0), 0
+        ),
         lax.all_gather(w_value, "seq", axis=0, tiled=True),
     )
     columns = normed

time: 833 us -> 774 us (0.929)
  waiting for transfers between devices: 615 us -> 546 us
    all_gather x1 -> x0, waiting for transfers between devices: 86.3 us -> none  [shards(): lax.all_gather(w_key, 'seq', axis=0, tiled=True)]
    all_to_all x0 -> x1, waiting for transfers between devices: none -> 28.9 us  [shards(): jax.lax.all_to_all(jnp.stack([w_key] * jax.lax.axis_size('seq'), 0), 'seq...]
    all_gather x1, waiting for transfers between devices: 101 us -> 89.4 us  [shards(): lax.all_gather(w_query, 'seq', axis=0, tiled=True)]
  transfers between devices with their start and end apart: 8 -> 8, of which waited for: 7 -> 7; matrix products, arithmetic and copies ran while one was open for 9% -> 11% of each run, Pallas kernels for 0% -> 0%
where the time goes in v1:
time: 774 us; the launch traced here: 772 us
  waiting for transfers between devices  546 us (71%)
  blocking collectives  103 us (13%)
  local copies, waits for them, and re-layouts  51.1 us (7%)
  matrix products  20.1 us (3%)
  other arithmetic  18.8 us (2%)
  between operations  15.9 us (2%)
  loops' own time  10.4 us (1%)
    all_gather x1, waiting for transfers between devices, shards(): key_piece = lax.all_gather(pf_key, 'seq', axis=0, tiled=True)  108 us
    all_gather x1, waiting for transfers between devices, shards(): lax.all_gather(w_output, 'seq', axis=0, tiled=True)  104 us
    all_gather x1, blocking collectives, combined_all(): lax.all_gather(part.astype(kind), axis)  103 us
    all_gather x1, waiting for transfers between devices, shards(): lax.all_gather(w_value, 'seq', axis=0, tiled=True)  95.4 us
    all_gather x1, waiting for transfers between devices, shards(): lax.all_gather(w_query, 'seq', axis=0, tiled=True)  89.4 us
    all_gather x1, waiting for transfers between devices, combined_all(): lax.all_gather(part.astype(kind), axis)  75.6 us
    all_gather x1, waiting for transfers between devices, shards(): heads_all = lax.all_gather(attn_rows, 'tp', axis=1, tiled=True)  42.5 us
    all_to_all x1, waiting for transfers between devices, shards(): jax.lax.all_to_all(jnp.stack([w_key] * jax.lax.axis_size('seq'), 0), 'seq...  28.9 us
  transfers between devices with their start and end apart: 8, of which 7 were waited for; matrix products, arithmetic and copies ran while one was open for 11% of the time, Pallas kernels for 0%

profile of v1, /device:TPU:2, one launch (start us, length us, event | category | flops | bytes accessed | tf_op | source)
XLA Modules:
  0.0 771.9 jit_solution(4925697310129615887)
XLA Ops:
  8.7 2.5 fusion.4
  11.3 95.4 %all-gather.12.cloned.1.call-done = bf16[4608,256]{1,0:T(8,128)(2,1)} async-done(((bf16[144,256]{1,0:T(8,128)(2,1)}), bf16[4608,256]{1,0:T(8,128)(2,1)}) %all-gather.12.cloned.1.call-update) | async-done | bytes 2359312 | tf_op jit(solution)/shard_map/all_gather | solution.py:127
  106.7 2.6 convolution_convert_fusion.1
  110.1 1.6 stack.2
  111.7 6.2 all-to-all-start
  119.2 28.9 %all-to-all-done = bf16[32,144,256]{2,1,0:T(8,128)(2,1)S(1)} async-done(((bf16[32,144,256]{2,1,0:T(8,128)(2,1)}), bf16[32,144,256]{2,1,0:T(8,128)(2,1)S(1)}, u32[]{:S(2)}, u32[]{:S(2)}) %all-to-all-start) | async-done | bytes 2359328 | tf_op jit(solution)/shard_map/all_to_all | solution.py:125
  148.1 2.5 copy.167
  150.6 3.4 fusion.7
  155.9 1.7 reshape.532
  157.6 1.0 reshape.536
  158.7 1.0 reshape.534
  162.4 1.2 broadcast_compare_fusion
  163.7 89.4 %all-gather.10.cloned.1.call-done = bf16[4608,512]{1,0:T(8,128)(2,1)} async-done(((bf16[144,512]{1,0:T(8,128)(2,1)}), bf16[4608,512]{1,0:T(8,128)(2,1)}) %all-gather.10.cloned.1.call-update) | async-done | bytes 4718608 | tf_op jit(solution)/shard_map/all_gather | solution.py:123
  253.1 5.1 fusion.59
  258.2 1.3 reshape.524
  267.8 103.1 %all_gather.30 = bf16[32,64,2,2]{1,3,2,0:T(2,128)(2,1)S(1)} all-gather(bf16[1,64,2,2]{1,3,2,0:T(2,128)(2,1)S(1)} %add_convert_fusion.2), channel_id=1, replica_groups=mesh['seq'=32,'tp'=8] {'seq'}, dimensions={0}, use_global_device_ids=true | all-gather | bytes 16896 | tf_op jit(solution)/shard_map/all_gather | solution.py:18
  371.2 6.4 copy.171
  377.6 108.3 %all-gather.8.cloned.1.call-done = bf16[8192,256]{0,1:T(8,128)(2,1)} async-done(((bf16[256,256]{0,1:T(8,128)(2,1)}), bf16[8192,256]{0,1:T(8,128)(2,1)}) %all-gather.8.cloned.1.call-update) | async-done | bytes 4194320 | tf_op jit(solution)/shard_map/all_gather | solution.py:151
  485.9 13.3 %while.34 = (s32[]{:T(128)}, f32[256,2,2]{0,2,1:T(2,128)S(1)}, f32[256,2,2,128]{3,0,2,1:T(8,128)S(1)}, s32[]{:T(128)}, s32[]{:T(128)}, /*index=5*/s32[256]{0:T(2...) while((s32[]{:T(128)}, f32[256,2,2]{0,2,1:T(2,128)S(1)}, ...), condition=%wide.region_12.13_spmd.clone, body=%wide.region_6.12_spmd.clone.sunk | while | flops 271590688 | bytes 5275049 | solution.py:189
  489.1 3.1 conditional.3
  489.1 1.1 constant_dynamic-slice_fusion
  490.7 0.9 fusion.62
  499.4 75.6 %all-gather.16.cloned.1.call-done = bf16[32,64,2,2,128]{4,1,3,2,0:T(8,128)(2,1)} async-done(((bf16[1,64,2,2,128]{4,1,3,2,0:T(8,128)(2,1)}), bf16[32,64,2,2,128]{4,1,3,2,0:T(8,128)(2,1)}) %all-gather.16.cloned.1.call-update) | async-done | bytes 2097168 | tf_op jit(solution)/shard_map/all_gather | solution.py:18
  576.0 33.7 %while.33 = (s32[]{:T(128)}, f32[64,2,2]{0,2,1:T(2,128)S(1)}, f32[64,2,2,128]{3,2,1,0:T(2,128)S(1)}, bf16[32,64,2,2]{1,3,2,0:T(2,128)(2,1)S(1)}, bf16[32,64,2,2,...) while((s32[]{:T(128)}, f32[64,2,2]{0,2,1:T(2,128)S(1)}, f32[64,2,2,128]{3,2,1,0:T(2,128)S(1)}, ...), condition=%wide.region_19.20_spmd, body=%wide.region_18.19_spmd.sunk | while | flops 66053 | bytes 461447 | solution.py:26
  584.7 0.9 constant_dynamic-slice_fusion.5
  585.8 0.9 constant_dynamic-slice_fusion.5
  586.9 0.9 constant_dynamic-slice_fusion.5
  590.2 0.9 constant_dynamic-slice_fusion.5
  611.1 104.0 %all-gather.20.cloned.1.call-done = bf16[4096,576]{0,1:T(8,128)(2,1)} async-done(((bf16[128,576]{0,1:T(8,128)(2,1)}), bf16[4096,576]{0,1:T(8,128)(2,1)}) %all-gather.20.cloned.1.call-update) | async-done | bytes 4718608 | tf_op jit(solution)/shard_map/all_gather | solution.py:273
  715.1 42.5 %all-gather.18.cloned.1.call-done = bf16[258,4096]{0,1:T(8,128)(2,1)} async-done(((bf16[258,512]{0,1:T(8,128)(2,1)}), bf16[258,4096]{0,1:T(8,128)(2,1)}) %all-gather.18.cloned.1.call-update) | async-done | bytes 2113552 | tf_op jit(solution)/shard_map/all_gather | solution.py:269
  757.6 5.9 convolution_convert_fusion
  764.1 0.9 copy.193
  (261 shorter events, 49.9 us)
Async XLA Ops:
  7.2 99.5 %copy-start.2 = (bf16[64,4608]{1,0:T(8,128)(2,1)S(1)}, bf16[64,4608]{1,0:T(8,128)(2,1)}, u32[]{:S(2)}) copy-start(bf16[64,4608]{1,0:T(8,128)(2,1)} %param.24) | copy-start | bytes 1769476
  7.2 99.5 %copy-start = (bf16[256,4608]{1,0:T(8,128)(2,1)S(1)}, bf16[256,4608]{1,0:T(8,128)(2,1)}, u32[]{:S(2)}) copy-start(bf16[256,4608]{1,0:T(8,128)(2,1)} %param.23) | copy-start | bytes 7077892
  7.2 99.5 %copy-start.18 = (f32[4608]{0:T(1024)S(1)}, f32[4608]{0:T(1024)}, u32[]{:S(2)}) copy-start(f32[4608]{0:T(1024)} %param.25) | copy-start | bytes 55300
  7.2 99.5 %all-gather.12.cloned.1.call-start = ((), (), s32[]{:S(2)}) async-start(), calls=%async_computation.3 | async-start | bytes 2433024 | tf_op jit(solution)/shard_map/all_gather | solution.py:127
  7.9 245.1 %all-gather.10.cloned.1.call-start = ((), (), s32[]{:S(2)}) async-start(), calls=%async_computation.2 | async-start | bytes 4866048 | tf_op jit(solution)/shard_map/all_gather | solution.py:123
  8.7 362.5 %all-gather.14.cloned.1.call-start = ((), (), s32[]{:S(2)}) async-start(), calls=%async_computation.4 | async-start | bytes 4325376 | tf_op jit(solution)/shard_map/all_gather | solution.py:152
  11.3 139.3 %copy-start.8 = (f32[320]{0:T(512)}, f32[320]{0:T(512)S(1)}, u32[]{:S(2)}) copy-start(f32[320]{0:T(512)S(1)} %add_rsqrt_fusion) | copy-start | bytes 3844
  11.3 98.8 %copy-start.7 = (bf16[144,256]{1,0:T(8,128)(2,1)S(1)}, bf16[144,256]{1,0:T(8,128)(2,1)}, u32[]{:S(2)}) copy-start(bf16[144,256]{1,0:T(8,128)(2,1)} %param.27) | copy-start | bytes 221188
  109.4 2.4 copy-start.6
  110.1 7.9 %copy-start.16 = (s32[6]{0:T(128)S(1)}, s32[6]{0:T(128)}, u32[]{:S(2)}) copy-start(s32[6]{0:T(128)} %param.30) | copy-start | bytes 76
  110.1 8.1 %copy-start.10 = (s32[2]{0:T(128)S(1)}, s32[2]{0:T(128)}, u32[]{:S(2)}) copy-start(s32[2]{0:T(128)} %param.31) | copy-start | bytes 28
  110.1 8.2 %copy-start.11 = (s32[32]{0:T(128)S(1)}, s32[32]{0:T(128)}, u32[]{:S(2)}) copy-start(s32[32]{0:T(128)} %param.32) | copy-start | bytes 388
  111.7 36.3 %all-to-all-start = ((bf16[32,144,256]{2,1,0:T(8,128)(2,1)}), bf16[32,144,256]{2,1,0:T(8,128)(2,1)S(1)}, u32[]{:S(2)}, u32[]{:S(2)}) async-start(bf16[32,144,256]{2,1,0:T(8,128)(2,1)} %stack.2), calls=%async_computation | async-start | bytes 4718592 | tf_op jit(solution)/shard_map/all_to_all | solution.py:125
  117.9 367.9 %all-gather.8.cloned.1.call-start = ((), (), s32[]{:S(2)}) async-start(), calls=%async_computation.1 | async-start | bytes 4325376 | tf_op jit(solution)/shard_map/all_gather | solution.py:151
  150.6 4.6 copy-start.3
  154.0 6.3 copy-start.12
  154.0 99.1 %copy-start.1 = (bf16[256,4608]{1,0:T(8,128)(2,1)S(1)}, bf16[256,4608]{1,0:T(8,128)(2,1)}, u32[]{:S(2)}) copy-start(bf16[256,4608]{1,0:T(8,128)(2,1)} %param.23) | copy-start | bytes 7077892
  155.1 419.9 %all-gather.16.cloned.1.call-start = ((), (), s32[]{:S(2)}) async-start(), calls=%async_computation.5 | async-start | bytes 2162688 | tf_op jit(solution)/shard_map/all_gather | solution.py:18
  160.3 0.8 copy-start.14
  259.9 0.7 copy-start.13
  259.9 0.7 copy-start.15
  259.9 1.0 copy-start.5
  259.9 0.9 copy-start.19
  260.0 1.6 copy-start.4
  260.0 1.6 copy-start.9
  260.1 4.7 copy-start.20
  260.1 6.0 slice-start
  262.8 452.4 %all-gather.20.cloned.1.call-start = ((), (), s32[]{:S(2)}) async-start(), calls=%async_computation.7 | async-start | bytes 4866048 | tf_op jit(solution)/shard_map/all_gather | solution.py:273
  263.3 494.3 %all-gather.18.cloned.1.call-start = ((), (), s32[]{:S(2)}) async-start(), calls=%async_computation.6 | async-start | bytes 3538944 | tf_op jit(solution)/shard_map/all_gather | solution.py:269
  371.2 114.7 %copy-start.17 = (s32[6]{0:T(128)S(1)}, s32[6]{0:T(128)}, u32[]{:S(2)}) copy-start(s32[6]{0:T(128)} %param.30) | copy-start | bytes 76
Sparse Core Ops, SparseCore 0:
  11.4 95.2 all-gather.11
  110.1 142.9 all-gather.9
  256.5 105.5 all-gather.13
  365.2 120.6 all-gather.7
  489.7 85.2 all-gather.15
  578.1 136.9 all-gather.19
  716.9 40.6 all-gather.17
